TPU v7x, 128 devices: a whole 4x4x4 slice. The times are simulated.
128 devices in a mesh: section: 2 (over core), seq: 64 (over z, x, y).
Axes of the slice: x: 4, y: 4, z: 4, core: 2. Of those that a mesh axis runs over, the one named last changes fastest.
Arguments:
- patches: bfloat16 [32768, 1408], P('seq'), may hold values from -42 to 42
- image_grid: int32 [256, 2], P('seq'), may hold values from 2 to 52, as said below
- image_offsets: int32 [256], P('seq'), may hold values from 0 to 32736, as said below
- dest_positions: int32 [8192], replicated, may hold values from 0 to 16383, as said below
- text_embeds: bfloat16 [256, 64, 1408], P(None, 'seq'), may hold values from -42 to 42
- segment_ids: int32 [256, 64], replicated, may hold values from 0 to 3, as said below
- vision_qkv: bfloat16 [1408, 3, 1408], P(None, None, 'section'), may hold values from -0.15625 to 0.15625
- vision_out: bfloat16 [1408, 1408], P('section'), may hold values from -0.875 to 0.875
- projector: bfloat16 [4, 1408, 1408], P('section'), may hold values from -0.078125 to 0.078125
- decoder_q: bfloat16 [1408, 1408], P(None, 'section'), may hold values from -0.15625 to 0.15625
- decoder_kv: bfloat16 [1408, 2, 176], P(None, None, 'section'), may hold values from -0.15625 to 0.15625
- decoder_out: bfloat16 [1408, 1408], P('section'), may hold values from -0.875 to 0.875
Outputs:
- decoded: bfloat16 [256, 64, 1408], P(None, 'seq')
Inputs may be any that keep to these rules, and one draw needn't show every extreme that they name: `image_grid`: patch rows and columns are even, columns are 8 or 16; the images of one index of seq lie back to back and cover exactly its 512 patches. `image_offsets`: each image's first patch; images are in order, back to back, the first of an index of seq at its first patch. `dest_positions`: the 128 merged rows of one index of seq go, in order, to 128 consecutive prompt positions; the ranges of different indices do not meet. `segment_ids`: never falls along prompt positions; every document number is used.
All inputs are finite; a program needn't handle non-finite values.
Results may differ from a plain program's by a relative error of at most 0.025.
Values may be sent and summed in bfloat16 or wider, within the bound.
No kernel may reach another device: no remote copies, remote signals or barrier semaphores. Data moves between devices by JAX's collectives and lax.ppermute only.
A program may use at most 128 MiB of HBM per device.

v0:
```python
import math
import jax
import jax.numpy as jnp
from jax import lax
from jax.sharding import PartitionSpec as P

D = 1408
HEAD = 88
CHUNKS = 4


def layer_norm(values):
    values = values.astype(jnp.float32)
    centred = values - jnp.mean(values, -1, keepdims=True)
    return centred * lax.rsqrt(jnp.mean(centred * centred, -1, keepdims=True) + 1e-06)


def root_norm(values):
    values = values.astype(jnp.float32)
    return values * lax.rsqrt(jnp.mean(values * values, -1, keepdims=True) + 1e-06)


def merge_rows(grid, offsets, count):
    heights = grid[:, 0]
    widths = grid[:, 1]
    group_start = offsets // 4
    group_count = heights * widths // 4
    merged_ids = jnp.arange(count, dtype=jnp.int32)
    inside = (
        (merged_ids[:, None] >= group_start[None, :])
        & (merged_ids[:, None] < (group_start + group_count)[None, :])
    ).astype(jnp.int32)
    first_group = jnp.sum(inside * group_start[None, :], 1)
    first_patch = jnp.sum(inside * offsets[None, :], 1)
    row_width = jnp.sum(inside * widths[None, :], 1)
    within = merged_ids - first_group
    groups_across = row_width // 2
    group_row = within // groups_across
    group_col = within % groups_across
    corner = first_patch + 2 * group_row * row_width + 2 * group_col
    return jnp.stack([corner, corner + 1, corner + row_width, corner + row_width + 1], 1)


def swap(values):
    return lax.ppermute(values, "section", [(0, 1), (1, 0)])


def in_head_order(first, own, other, axis):
    return jnp.where(
        first, jnp.concatenate([own, other], axis), jnp.concatenate([other, own], axis)
    )


def body(
    patches,
    image_grid,
    image_offsets,
    dest_positions,
    text_embeds,
    segment_ids,
    vision_qkv,
    vision_out,
    projector,
    decoder_q,
    decoder_kv,
    decoder_out,
):
    section_index = lax.axis_index("section")
    seq_index = lax.axis_index("seq")
    seq_count = lax.axis_size("seq")
    first = section_index == 0
    scale = 3.0 / math.sqrt(HEAD)
    patch_count = patches.shape[0]
    local_heads = vision_out.shape[0] // HEAD
    merged_count = patch_count // 4
    vision_out_other = swap(vision_out)
    decoder_out_full = in_head_order(first, decoder_out, swap(decoder_out), 0)
    normed = layer_norm(patches).astype(jnp.bfloat16)
    mixed = jnp.dot(normed, vision_qkv.reshape(D, -1), preferred_element_type=jnp.float32).reshape(
        patch_count, 3, local_heads, HEAD
    )
    queries = root_norm(mixed[:, 0]).astype(jnp.bfloat16)
    keys = root_norm(mixed[:, 1]).astype(jnp.bfloat16)
    values = mixed[:, 2].astype(jnp.bfloat16)
    offsets = image_offsets - seq_index * patch_count
    image_of = jnp.sum(
        (jnp.arange(patch_count, dtype=jnp.int32)[:, None] >= offsets[None, :]).astype(jnp.int32), 1
    )
    scores = jnp.einsum("qhd,khd->hqk", queries, keys, preferred_element_type=jnp.float32) * scale
    same = (image_of[:, None] == image_of[None, :])[None]
    weights = jnp.where(same, jnp.exp(scores), jnp.zeros_like(scores))
    totals = jnp.sum(weights, -1)
    mixed_values = jnp.einsum(
        "hqk,khd->qhd", weights.astype(jnp.bfloat16), values, preferred_element_type=jnp.float32
    )
    attended = (
        (mixed_values / jnp.transpose(totals)[:, :, None])
        .astype(jnp.bfloat16)
        .reshape(patch_count, local_heads * HEAD)
    )
    picks = merge_rows(image_grid, offsets, merged_count)
    own_picks = lax.dynamic_slice_in_dim(picks, 2 * section_index, 2, 1).reshape(-1)
    other_picks = lax.dynamic_slice_in_dim(picks, 2 - 2 * section_index, 2, 1).reshape(-1)
    received_heads = swap(attended[other_picks])
    own_rows = jnp.concatenate([attended[own_picks], received_heads], 1)
    full_out = jnp.concatenate([vision_out, vision_out_other], 0)
    kept = (
        patches[own_picks].astype(jnp.float32)
        + jnp.dot(own_rows, full_out, preferred_element_type=jnp.float32)
    ).astype(jnp.bfloat16)
    merge_terms = jnp.dot(
        kept.reshape(merged_count, 2 * D),
        projector.reshape(2 * D, D),
        preferred_element_type=jnp.float32,
    )
    image_rows = (merge_terms + swap(merge_terms)).astype(jnp.bfloat16)
    per_peer = merged_count // seq_count
    run_starts = dest_positions.reshape(seq_count, merged_count)[:, 0]
    own_start = run_starts[seq_index]
    received = lax.all_to_all(
        jnp.roll(image_rows.reshape(per_peer, seq_count, image_rows.shape[1]), own_start, axis=1),
        "seq",
        split_axis=1,
        concat_axis=1,
        tiled=True,
    )
    slot_base = jnp.arange(per_peer, dtype=jnp.int32)[:, None] * seq_count
    landing = (
        run_starts[None, :] + slot_base + (seq_index - run_starts[None, :]) % seq_count
    ) // seq_count
    text_rows = text_embeds.shape[0]
    prompt = text_embeds.reshape(text_rows, D).at[landing.reshape(-1)].set(received.reshape(-1, D))
    text_normed = root_norm(prompt).astype(jnp.bfloat16)
    text_queries = root_norm(
        jnp.dot(text_normed, decoder_q, preferred_element_type=jnp.float32).reshape(
            text_rows, local_heads, HEAD
        )
    ).astype(jnp.bfloat16)
    paired = jnp.dot(
        text_normed, decoder_kv.reshape(D, -1), preferred_element_type=jnp.float32
    ).reshape(text_rows, 2, HEAD)
    key_rows = root_norm(paired[:, 0]).astype(jnp.bfloat16)
    value_rows = paired[:, 1].astype(jnp.bfloat16)
    shared = jnp.stack([key_rows, value_rows], 1)
    query_places = jnp.arange(text_rows, dtype=jnp.int32) * seq_count + seq_index
    query_segments = lax.dynamic_slice_in_dim(segment_ids, seq_index, 1, 1)[:, 0]
    step = text_rows // CHUNKS
    sums = jnp.zeros((text_rows, local_heads, HEAD), jnp.float32)
    totals = jnp.zeros((text_rows, local_heads), jnp.float32)
    for chunk in range(CHUNKS):
        low = chunk * step
        piece = lax.all_gather(shared[None, low : low + step], "seq", axis=0, tiled=True)
        piece = piece.reshape(seq_count * step, 2, HEAD)
        key_places = (
            jnp.arange(seq_count, dtype=jnp.int32)[:, None]
            + (low + jnp.arange(step, dtype=jnp.int32))[None, :] * seq_count
        ).reshape(-1)
        key_segments = jnp.transpose(segment_ids[low : low + step]).reshape(-1)
        chunk_queries = text_queries[low:]
        scores = (
            jnp.einsum(
                "qgd,ld->qgl", chunk_queries, piece[:, 0], preferred_element_type=jnp.float32
            )
            * scale
        )
        allowed = (key_places[None, :] <= query_places[low:, None]) & (
            key_segments[None, :] == query_segments[low:, None]
        )
        weights = jnp.where(allowed[:, None, :], jnp.exp(scores), jnp.zeros_like(scores))
        totals = totals.at[low:].add(jnp.sum(weights, -1))
        sums = sums.at[low:].add(
            jnp.einsum(
                "qgl,ld->qgd",
                weights.astype(jnp.bfloat16),
                piece[:, 1],
                preferred_element_type=jnp.float32,
            )
        )
    attended_text = (sums / totals[..., None]).astype(jnp.bfloat16).reshape(text_rows, -1)
    all_heads = in_head_order(first, attended_text, swap(attended_text), 1)
    output_terms = jnp.dot(all_heads, decoder_out_full, preferred_element_type=jnp.float32)
    decoded = (prompt.astype(jnp.float32) + output_terms).astype(jnp.bfloat16)
    return decoded.reshape(text_rows, 1, D)


def solution(mesh):
    placed = (
        P("seq", None),
        P("seq", None),
        P("seq"),
        P(),
        P(None, "seq", None),
        P(),
        P(None, None, "section"),
        P("section", None),
        P("section", None, None),
        P(None, "section"),
        P(None, None, "section"),
        P("section", None),
    )
    return jax.shard_map(
        body, mesh=mesh, in_specs=placed, out_specs=P(None, "seq", None), check_vma=False
    )
```

profile of v0, /device:TPU:1, one launch (start us, length us, event | category | flops | bytes accessed | tf_op | source)
XLA Modules:
  0.0 394.0 jit_solution(17752541069491407956)
XLA Ops:
  6.5 1.4 collective-permute-start.1
  8.0 0.7 slice_bitcast_fusion.6
  8.6 0.8 fusion.109
  9.7 0.9 broadcast_compare_fusion
  10.7 1.6 convert_reduce_fusion
  12.3 0.5 fusion.40
  12.8 6.0 %fusion.57 = f32[512,3,8,88]{0,3,2,1:T(8,128)S(1)} fusion(bf16[3,8,88,1408]{3,2,1,0:T(8,128)(2,1)} %bitcast.178, bf16[512,1408]{1,0:T(8,128)(2,1)S(1)} %copy-done.2, f32[512]{0:T(512)S(1)} %add_rsqrt_fusion.3, f32[512]{0:T(512)S(1)} %broadcast_multiply_fusion), kind=kOutput, calls=%fused_computation.63 | convolution fusion | flops 3047948288 | bytes 11718656 | tf_op jit(solution)/shard_map/dot_general | solution.py:79
  18.8 2.0 copy-done.4
  21.8 4.2 %fusion.15 = (f32[8,512]{1,0:T(8,128)S(1)}, f32[8,512,512]{1,2,0:T(8,128)S(1)}) fusion(pred[512,512]{0,1:T(8,128)(4,1)} %broadcast_compare_fusion, f32[512,3,8,88]{0,3,2,1:T(8,128)} %copy-done.4, f32[512,8]{0,1:T(8,128)S(1)} %get-tuple-element.165, f32[512,8]{0,1:T(8,128)S(1)} %get-tuple-element.166), kind=kOutput, calls=%fused_computation.21 | convolution fusion | flops 376827904 | bytes 11583488 | tf_op jit(solution)/shard_map/qhd,khd->hqk/dot_general | solution.py:89
  26.1 3.1 divide_convert_fusion
  29.5 1.2 gather_fusion.2
  30.7 0.4 collective-permute-start
  31.1 4.3 %gather_fusion = bf16[256,1408]{1,0:T(8,128)(2,1)} fusion(bf16[512,1408]{1,0:T(8,128)(2,1)} %param.32, s32[1024]{0:T(1024)S(1)} %pad_clamp_fusion.1), kind=kCustom, calls=%fused_computation | custom fusion | bytes 1442816 | tf_op jit(solution)/shard_map/gather | solution.py:108
  35.4 1.9 gather_fusion.1
  37.3 4.0 %fusion.46 = bf16[256,1408]{1,0:T(8,128)(2,1)S(1)} fusion(bf16[704,1408]{1,0:T(8,128)(2,1)} %collective-permute-done.1, bf16[704,1408]{1,0:T(8,128)(2,1)} %param.39, bf16[256,1408]{1,0:T(8,128)(2,1)} %gather_fusion, bf16[256,704]{1,0:T(8,128)(2,1)} %collective-permute-done, bf16[256,704]{1,0:T(8,128)(2,1)} %gather_fusion.1), kind=kOutput, calls=%fused_computation.53 | convolution fusion | flops 1025474560 | bytes 6127616 | tf_op jit(solution)/shard_map/dot_general | solution.py:109
  41.6 4.5 %fusion.128 = f32[128,1408]{1,0:T(8,128)S(1)} fusion(bf16[128,2816]{1,0:T(8,128)(2,1)S(1)} %reshape.1031, bf16[2816,1408]{1,0:T(8,128)(2,1)} %bitcast.163), kind=kOutput, calls=%fused_computation.233 | convolution fusion | flops 1015021568 | bytes 9371648 | tf_op jit(solution)/shard_map/dot_general | solution.py:111
  46.7 0.5 constant_dynamic-slice_fusion.1
  49.2 1.2 add_convert_fusion
  50.7 1.7 fusion.96
  52.4 11.2 %all-to-all-start = ((bf16[2,64,1408]{2,0,1:T(2,128)(2,1)}), bf16[2,64,1408]{2,0,1:T(2,128)(2,1)S(1)}, u32[]{:S(2)}, u32[]{:S(2)}) async-start(bf16[2,64,1408]{2,0,1:T(2,128)(2,1)} %fusion.96), calls=%async_computation | async-start | bytes 720896 | tf_op jit(solution)/shard_map/all_to_all | solution.py:120
  63.9 10.6 %all-to-all-done = bf16[2,64,1408]{2,0,1:T(2,128)(2,1)S(1)} async-done(((bf16[2,64,1408]{2,0,1:T(2,128)(2,1)}), bf16[2,64,1408]{2,0,1:T(2,128)(2,1)S(1)}, u32[]{:S(2)}, u32[]{:S(2)}) %all-to-all-start) | async-done | bytes 360480 | tf_op jit(solution)/shard_map/all_to_all | solution.py:120
  74.5 1.6 scatter_fusion
  76.3 1.5 fusion.89
  78.0 0.7 copy.106
  78.8 1.8 collective-permute-start.4
  81.0 0.7 copy.110
  82.1 1.0 compare_and_fusion.3
  83.0 1.3 compare_and_fusion.2
  84.3 0.7 copy.114
  85.5 1.6 compare_and_fusion.1
  87.2 1.9 compare_and_fusion
  89.1 0.8 fusion.98
  90.5 0.8 fusion.91
  91.7 0.8 copy.118
  92.6 48.0 %all-gather.9.cloned.1.call-done = bf16[4096,2,88]{2,1,0:T(2,128)(2,1)} async-done(((bf16[64,2,88]{2,1,0:T(2,128)(2,1)}), bf16[4096,2,88]{2,1,0:T(2,128)(2,1)}) %all-gather.9.cloned.1.call-update) | async-done | bytes 1441808 | tf_op jit(solution)/shard_map/all_gather | solution.py:152
  140.6 7.2 %fusion.126 = (bf16[4096,1,88]{2,1,0:T(2,128)(2,1)}, bf16[4096,1,88]{2,1,0:T(2,128)(2,1)}) fusion(bf16[4096,2,88]{2,1,0:T(2,128)(2,1)} %all-gather.9.cloned.1.call-done), kind=kLoop, calls=%fused_computation.231 | loop fusion | bytes 2883584 | tf_op jit(solution)/shard_map/slice | solution.py:175
  147.8 5.3 %copy.126 = bf16[4096,1,88]{0,2,1:T(8,128)(2,1)} copy(bf16[4096,1,88]{2,1,0:T(2,128)(2,1)} %get-tuple-element.138) | data formatting | bytes 1441792
  153.0 5.3 %copy.127 = bf16[4096,1,88]{0,2,1:T(8,128)(2,1)} copy(bf16[4096,1,88]{2,1,0:T(2,128)(2,1)} %get-tuple-element.137) | data formatting | bytes 1441792
  158.3 48.3 %all-gather.11.cloned.1.call-done = bf16[4096,2,88]{2,1,0:T(2,128)(2,1)} async-done(((bf16[64,2,88]{2,1,0:T(2,128)(2,1)}), bf16[4096,2,88]{2,1,0:T(2,128)(2,1)}) %all-gather.11.cloned.1.call-update) | async-done | bytes 1441808 | tf_op jit(solution)/shard_map/all_gather | solution.py:152
  206.6 6.9 %fusion.125 = (bf16[4096,1,88]{2,1,0:T(2,128)(2,1)}, bf16[4096,1,88]{2,1,0:T(2,128)(2,1)}) fusion(bf16[4096,2,88]{2,1,0:T(2,128)(2,1)} %all-gather.11.cloned.1.call-done), kind=kLoop, calls=%fused_computation.230 | loop fusion | bytes 2883584 | tf_op jit(solution)/shard_map/slice | solution.py:175
  213.5 4.7 %copy.128 = bf16[4096,1,88]{0,2,1:T(8,128)(2,1)S(1)} copy(bf16[4096,1,88]{2,1,0:T(2,128)(2,1)} %get-tuple-element.136) | data formatting | bytes 1441792
  218.2 5.3 %copy.129 = bf16[4096,1,88]{0,2,1:T(8,128)(2,1)} copy(bf16[4096,1,88]{2,1,0:T(2,128)(2,1)} %get-tuple-element.135) | data formatting | bytes 1441792
  223.5 12.1 %fusion.2 = (f32[192,8]{1,0:T(8,128)}, f32[192,8,4096]{2,1,0:T(8,128)}) fusion(pred[192,4096]{1,0:T(8,128)(4,1)S(1)} %copy-done.7, bf16[256,8,88]{2,1,0:T(8,128)(2,1)S(1)} %multiply_convert_fusion.2, bf16[4096,1,88]{0,2,1:T(8,128)(2,1)S(1)} %copy.128), kind=kOutput, calls=%fused_computation.8 | convolution fusion | flops 1126169088 | bytes 27039744 | tf_op jit(solution)/shard_map/qgd,ld->qgl/dot_general | solution.py:161
  235.6 10.5 %fusion.9 = f32[192,8,88]{2,1,0:T(8,128)S(1)} fusion(f32[192,8,4096]{2,1,0:T(8,128)} %get-tuple-element.158, pred[192,4096]{1,0:T(8,128)(4,1)S(1)} %copy-done.7, bf16[4096,1,88]{0,2,1:T(8,128)(2,1)} %copy.129), kind=kOutput, calls=%fused_computation.15 | convolution fusion | flops 1126170624 | bytes 27213824 | tf_op jit(solution)/shard_map/qgl,ld->qgd/dot_general | solution.py:172
  246.5 16.5 %fusion = (f32[256,8]{0,1:T(8,128)S(1)}, f32[256,8,4096]{2,0,1:T(8,128)}) fusion(pred[256,4096]{1,0:T(8,128)(4,1)} %compare_and_fusion, bf16[256,8,88]{0,2,1:T(8,128)(2,1)} %bitcast.170, bf16[4096,1,88]{0,2,1:T(8,128)(2,1)} %copy.126), kind=kOutput, calls=%fused_computation.5 | convolution fusion | flops 1501558784 | bytes 35692544 | tf_op jit(solution)/shard_map/qgd,ld->qgl/dot_general | solution.py:161
  263.0 13.8 %fusion.4 = f32[256,8,88]{0,2,1:T(8,128)S(1)} fusion(f32[256,8,4096]{2,0,1:T(8,128)} %get-tuple-element.156, pred[256,4096]{1,0:T(8,128)(4,1)S(1)} %copy-done.6, bf16[4096,1,88]{0,2,1:T(8,128)(2,1)S(1)} %copy-done.9), kind=kOutput, calls=%fused_computation.11 | convolution fusion | flops 1501560832 | bytes 36044800 | tf_op jit(solution)/shard_map/qgl,ld->qgd/dot_general | solution.py:172
  277.1 7.1 %scatter-add.20 = f32[256,8,88]{0,2,1:T(8,128)S(1)} dynamic-update-slice(f32[256,8,88]{0,2,1:T(8,128)S(1)} %fusion.4, f32[192,8,88]{0,2,1:T(8,128)S(1)} %slice_add_fusion, s32[]{:T(128)} %constant.358.clone.1, s32[]{:T(128)} %constant.360.clone.1, s32[]{:T(128)} %constant.360.clone.1) | dynamic-update-slice | bytes 1081348 | tf_op jit(solution)/shard_map/scatter-add | solution.py:171
  284.2 7.0 %fusion.124 = (bf16[4096,1,88]{2,1,0:T(2,128)(2,1)}, bf16[4096,1,88]{2,1,0:T(2,128)(2,1)}) fusion(bf16[4096,2,88]{2,1,0:T(2,128)(2,1)} %all-gather.13.cloned.1.call-done), kind=kLoop, calls=%fused_computation.229 | loop fusion | bytes 2883584 | tf_op jit(solution)/shard_map/slice | solution.py:175
  291.2 5.3 %copy.131 = bf16[4096,1,88]{0,2,1:T(8,128)(2,1)} copy(bf16[4096,1,88]{2,1,0:T(2,128)(2,1)} %get-tuple-element.133) | data formatting | bytes 1441792
  296.4 5.3 %copy.130 = bf16[4096,1,88]{0,2,1:T(8,128)(2,1)} copy(bf16[4096,1,88]{2,1,0:T(2,128)(2,1)} %get-tuple-element.134) | data formatting | bytes 1441792
  301.8 36.9 %all-gather.15.cloned.1.call-done = bf16[4096,2,88]{2,1,0:T(2,128)(2,1)} async-done(((bf16[64,2,88]{2,1,0:T(2,128)(2,1)}), bf16[4096,2,88]{2,1,0:T(2,128)(2,1)}) %all-gather.15.cloned.1.call-update) | async-done | bytes 1441808 | tf_op jit(solution)/shard_map/all_gather | solution.py:152
  338.7 6.8 %fusion.123 = (bf16[4096,1,88]{2,1,0:T(2,128)(2,1)}, bf16[4096,1,88]{2,1,0:T(2,128)(2,1)}) fusion(bf16[4096,2,88]{2,1,0:T(2,128)(2,1)} %all-gather.15.cloned.1.call-done), kind=kLoop, calls=%fused_computation.228 | loop fusion | bytes 2883584 | tf_op jit(solution)/shard_map/slice | solution.py:175
  345.5 4.6 %copy.132 = bf16[4096,1,88]{0,2,1:T(8,128)(2,1)S(1)} copy(bf16[4096,1,88]{2,1,0:T(2,128)(2,1)} %get-tuple-element.132) | data formatting | bytes 1441792
  350.1 5.3 %copy.133 = bf16[4096,1,88]{0,2,1:T(8,128)(2,1)} copy(bf16[4096,1,88]{2,1,0:T(2,128)(2,1)} %get-tuple-element.131) | data formatting | bytes 1441792
  355.4 3.9 fusion.17
  359.4 2.5 fusion.23
  361.9 1.1 copy.121
  363.4 5.7 %fusion.7 = (f32[128,8]{0,1:T(8,128)S(1)}, f32[128,8,4096]{2,0,1:T(8,128)S(1)}) fusion(pred[128,4096]{1,0:T(8,128)(4,1)S(1)} %copy-done.11, bf16[4096,1,88]{0,2,1:T(8,128)(2,1)} %copy.130, bf16[128,8,88]{2,1,0:T(8,128)(2,1)S(1)} %slice-done), kind=kOutput, calls=%fused_computation.13 | convolution fusion | flops 750779392 | bytes 18206720 | tf_op jit(solution)/shard_map/qgd,ld->qgl/dot_general | solution.py:161
  369.2 2.8 constant_dynamic-update-slice_fusion.1
  372.2 5.0 %scatter-add.24 = f32[256,8,88]{0,2,1:T(8,128)S(1)} dynamic-update-slice(f32[256,8,88]{0,2,1:T(8,128)S(1)} %get-tuple-element.153, f32[64,8,88]{0,2,1:T(8,128)S(1)} %slice_add_fusion.1, s32[]{:T(128)} %constant.377.clone.1, s32[]{:T(128)} %constant.360.clone.1, s32[]{:T(128)} %constant.360.clone.1) | dynamic-update-slice | bytes 360452 | tf_op jit(solution)/shard_map/scatter-add | solution.py:171
  377.6 0.7 copy-done.12
  378.3 1.6 collective-permute-start.3
  380.0 1.3 collective-permute-done.3
  381.3 6.0 %fusion.50 = bf16[256,1,1408]{2,0,1:T(8,128)(2,1)} fusion(bf16[704,1408]{1,0:T(8,128)(2,1)} %collective-permute-done.4, bf16[704,1408]{1,0:T(8,128)(2,1)} %param.43, pred[]{:T(512)S(6)} %eq.136, bf16[256,1408]{1,0:T(8,128)(2,1)S(1)} %scatter_fusion, bf16[256,704]{0,1:T(8,128)(2,1)S(1)} %collective-permute-done.3, bf16[256,704]{0,1:T(8,128)(2,1)} %bitcast.172), kind=kOutput, calls=%fused_computation.55 | convolution fusion | flops 1037189120 | bytes 6127617 | tf_op jit(solution)/shard_map/dot_general | solution.py:181
  (125 shorter events, 7.3 us)
Async XLA Ops:
  6.5 82.6 %copy-start = (bf16[1408,704]{0,1:T(8,128)(2,1)S(1)}, bf16[1408,704]{0,1:T(8,128)(2,1)}, u32[]{:S(2)}) copy-start(bf16[1408,704]{0,1:T(8,128)(2,1)} %param.41) | copy-start | bytes 5947396
  6.5 5.8 %copy-start.2 = (bf16[512,1408]{1,0:T(8,128)(2,1)S(1)}, bf16[512,1408]{1,0:T(8,128)(2,1)}, u32[]{:S(2)}) copy-start(bf16[512,1408]{1,0:T(8,128)(2,1)} %param.32) | copy-start | bytes 4325380
  6.5 30.8 %collective-permute-start.1 = (bf16[704,1408]{1,0:T(8,128)(2,1)}, bf16[704,1408]{1,0:T(8,128)(2,1)}, u32[]{:S(2)}, u32[]{:S(2)}) collective-permute-start(bf16[704,1408]{1,0:T(8,128)(2,1)} %param.39), channel_id=1, source_target_pairs={{0,64},{64,0},{1,65},{65,1},{2,66},{66,2},{3,67},{67,3},{4,68},{68... | collective-permute-start | bytes 5947400 | tf_op jit(solution)/shard_map/ppermute | solution.py:45
  18.8 2.0 copy-start.4
  21.8 4.2 %copy-start.15 = (pred[512,512]{0,1:T(8,128)(4,1)S(1)}, pred[512,512]{0,1:T(8,128)(4,1)}, u32[]{:S(2)}) copy-start(pred[512,512]{0,1:T(8,128)(4,1)} %broadcast_compare_fusion) | copy-start | bytes 786436
  30.7 6.6 %collective-permute-start = (bf16[256,704]{1,0:T(8,128)(2,1)S(1)}, bf16[256,704]{1,0:T(8,128)(2,1)}, u32[]{:S(2)}, u32[]{:S(2)}) collective-permute-start(bf16[256,704]{1,0:T(8,128)(2,1)S(1)} %gather_fusion.2), channel_id=1, source_target_pairs={{0,64},{64,0},{1,65},{65,1},{2,66},{66,2},{3,67},{67,3},{4,68},{68... | collective-permute-start | bytes 1081352 | tf_op jit(solution)/shard_map/ppermute | solution.py:45
  41.5 5.0 %copy-start.17 = (s32[8192]{0:T(1024)S(1)}, s32[8192]{0:T(1024)}, u32[]{:S(2)}) copy-start(s32[8192]{0:T(1024)} %param.35) | copy-start | bytes 98308
  46.1 28.4 %copy-start.3 = (bf16[256,1,1408]{2,0,1:T(8,128)(2,1)S(1)}, bf16[256,1,1408]{2,0,1:T(8,128)(2,1)}, u32[]{:S(2)}) copy-start(bf16[256,1,1408]{2,0,1:T(8,128)(2,1)} %param.36) | copy-start | bytes 2162692
  46.1 3.0 collective-permute-start.2
  52.4 22.1 %all-to-all-start = ((bf16[2,64,1408]{2,0,1:T(2,128)(2,1)}), bf16[2,64,1408]{2,0,1:T(2,128)(2,1)S(1)}, u32[]{:S(2)}, u32[]{:S(2)}) async-start(bf16[2,64,1408]{2,0,1:T(2,128)(2,1)} %fusion.96), calls=%async_computation | async-start | bytes 720896 | tf_op jit(solution)/shard_map/all_to_all | solution.py:120
  63.6 76.9 %all-gather.9.cloned.1.call-start = ((), (), s32[]{:S(2)}) async-start(), calls=%async_computation.1 | async-start | bytes 2129920 | tf_op jit(solution)/shard_map/all_gather | solution.py:152
  74.5 6.1 %copy-start.13 = (s32[256,64]{0,1:T(8,128)S(1)}, s32[256,64]{0,1:T(8,128)}, u32[]{:S(2)}) copy-start(s32[256,64]{0,1:T(8,128)} %param.37) | copy-start | bytes 196612
  78.8 127.9 %all-gather.11.cloned.1.call-start = ((), (), s32[]{:S(2)}) async-start(), calls=%async_computation.2 | async-start | bytes 2129920 | tf_op jit(solution)/shard_map/all_gather | solution.py:152
  78.8 301.1 %collective-permute-start.4 = (bf16[704,1408]{1,0:T(8,128)(2,1)}, bf16[704,1408]{1,0:T(8,128)(2,1)}, u32[]{:S(2)}, u32[]{:S(2)}) collective-permute-start(bf16[704,1408]{1,0:T(8,128)(2,1)} %param.43), channel_id=1, source_target_pairs={{0,64},{64,0},{1,65},{65,1},{2,66},{66,2},{3,67},{67,3},{4,68},{68... | collective-permute-start | bytes 5947400 | tf_op jit(solution)/shard_map/ppermute | solution.py:45
  81.7 202.5 %all-gather.13.cloned.1.call-start = ((), (), s32[]{:S(2)}) async-start(), calls=%async_computation.3 | async-start | bytes 2129920 | tf_op jit(solution)/shard_map/all_gather | solution.py:152
  85.0 253.6 %all-gather.15.cloned.1.call-start = ((), (), s32[]{:S(2)}) async-start(), calls=%async_computation.4 | async-start | bytes 2129920 | tf_op jit(solution)/shard_map/all_gather | solution.py:152
  91.7 263.7 %copy-start.5 = (bf16[256,8,88]{2,1,0:T(8,128)(2,1)}, bf16[256,8,88]{2,1,0:T(8,128)(2,1)S(1)}, u32[]{:S(2)}) copy-start(bf16[256,8,88]{2,1,0:T(8,128)(2,1)S(1)} %multiply_convert_fusion.2) | copy-start | bytes 1081348
  213.5 10.0 %copy-start.7 = (pred[192,4096]{1,0:T(8,128)(4,1)S(1)}, pred[192,4096]{1,0:T(8,128)(4,1)}, u32[]{:S(2)}) copy-start(pred[192,4096]{1,0:T(8,128)(4,1)} %compare_and_fusion.1) | copy-start | bytes 2359300
  246.5 16.5 %copy-start.6 = (pred[256,4096]{1,0:T(8,128)(4,1)S(1)}, pred[256,4096]{1,0:T(8,128)(4,1)}, u32[]{:S(2)}) copy-start(pred[256,4096]{1,0:T(8,128)(4,1)} %compare_and_fusion) | copy-start | bytes 3145732
  246.5 16.5 %copy-start.9 = (bf16[4096,1,88]{0,2,1:T(8,128)(2,1)S(1)}, bf16[4096,1,88]{0,2,1:T(8,128)(2,1)}, u32[]{:S(2)}) copy-start(bf16[4096,1,88]{0,2,1:T(8,128)(2,1)} %copy.127) | copy-start | bytes 2162692
  355.4 3.9 copy-start.10
  355.4 3.9 copy-start.14
  359.3 3.7 copy-start.16
  359.3 4.1 %slice-start = ((bf16[256,8,88]{2,1,0:T(8,128)(2,1)}), bf16[128,8,88]{2,1,0:T(8,128)(2,1)S(1)}, s32[]{:S(2)}) async-start(bf16[256,8,88]{2,1,0:T(8,128)(2,1)} %copy-done.5), calls=%async_computation.5 | async-start | bytes 524288 | tf_op jit(solution)/shard_map/slice | solution.py:159
  359.3 4.1 %copy-start.11 = (pred[128,4096]{1,0:T(8,128)(4,1)S(1)}, pred[128,4096]{1,0:T(8,128)(4,1)}, u32[]{:S(2)}) copy-start(pred[128,4096]{1,0:T(8,128)(4,1)} %compare_and_fusion.2) | copy-start | bytes 1572868
  363.4 5.7 %copy-start.8 = (bf16[4096,1,88]{0,2,1:T(8,128)(2,1)S(1)}, bf16[4096,1,88]{0,2,1:T(8,128)(2,1)}, u32[]{:S(2)}) copy-start(bf16[4096,1,88]{0,2,1:T(8,128)(2,1)} %copy.131) | copy-start | bytes 2162692
  377.6 0.7 copy-start.12
  378.3 2.9 collective-permute-start.3
  381.3 6.0 %copy-start.1 = (bf16[1408,704]{0,1:T(8,128)(2,1)S(1)}, bf16[1408,704]{0,1:T(8,128)(2,1)}, u32[]{:S(2)}) copy-start(bf16[1408,704]{0,1:T(8,128)(2,1)} %param.41) | copy-start | bytes 5947396
Sparse Core Ops, SparseCore 0:
  78.9 61.6 all-gather.8
  143.4 63.1 all-gather.10
  209.5 63.1 all-gather.12
  275.4 63.1 all-gather.14
where the time goes:
time: 401 us; the launch traced here: 394 us
  waiting for transfers between devices  145 us (36%)
  local copies, waits for them, and re-layouts  102 us (25%)
  matrix products  98 us (24%)
  starting transfers between devices  17 us (4%)
  between operations  15.9 us (4%)
  other arithmetic  15.7 us (4%)
    all_gather x4, waiting for transfers between devices, body(): lax.all_gather(shared[None, low:low + step], 'seq', axis=0, tiled=True)  133 us
    unnamed x44, local copies, waits for them, and re-layouts  43.9 us
    dot_general x4, matrix products, body(): jnp.einsum('qgd,ld->qgl', chunk_queries, piece[:, 0], preferred_element_t...  38.2 us
    dot_general x4, matrix products, body(): jnp.einsum('qgl,ld->qgd', weights.astype(jnp.bfloat16), piece[:, 1], pref...  29.7 us
    slice x4, local copies, waits for them, and re-layouts, body(): piece[:, 1]  27.8 us
    scatter-add x2, local copies, waits for them, and re-layouts, body(): sums.at[low:]  12.1 us
    all_to_all x1, starting transfers between devices, body(): lax.all_to_all(jnp.roll(image_rows.reshape(per_peer, seq_count, image_row...  11.2 us
    all_to_all x1, waiting for transfers between devices, body(): lax.all_to_all(jnp.roll(image_rows.reshape(per_peer, seq_count, image_row...  10.6 us
  transfers between devices with their start and end apart: 10, of which 5 were waited for; matrix products, arithmetic and copies ran while one was open for 48% of the time, Pallas kernels for 0%

commit v1 on v0

--- a/solution.py
+++ b/solution.py
@@ -117,12 +117,15 @@
     per_peer = merged_count // seq_count
     run_starts = dest_positions.reshape(seq_count, merged_count)[:, 0]
     own_start = run_starts[seq_index]
-    received = lax.all_to_all(
-        jnp.roll(image_rows.reshape(per_peer, seq_count, image_rows.shape[1]), own_start, axis=1),
-        "seq",
-        split_axis=1,
-        concat_axis=1,
-        tiled=True,
+
+    def meet_the_page(obj, ax_name="seq"):
+        answer = jax.lax.axis_size(ax_name)
+        vec_out = jnp.stack(jnp.split(obj, answer, axis=1))
+        piece_out = jax.lax.all_to_all(vec_out, split_axis=0, axis_name=ax_name, concat_axis=0)
+        return jnp.concatenate(piece_out, axis=1)
+
+    received = meet_the_page(
+        jnp.roll(image_rows.reshape(per_peer, seq_count, image_rows.shape[1]), own_start, axis=1)
     )
     slot_base = jnp.arange(per_peer, dtype=jnp.int32)[:, None] * seq_count
     landing = (

time: 401 us -> 439 us (1.095)
  local copies, waits for them, and re-layouts: 102 us -> 140 us
    unnamed x44 -> x107, local copies, waits for them, and re-layouts: 43.9 us -> 81.6 us
  transfers between devices with their start and end apart: 10 -> 10, of which waited for: 5 -> 5; matrix products, arithmetic and copies ran while one was open for 48% -> 44% of each run, Pallas kernels for 0% -> 0%
where the time goes in v1:
time: 439 us; the launch traced here: 432 us
  waiting for transfers between devices  145 us (33%)
  local copies, waits for them, and re-layouts  140 us (32%)
  matrix products  98 us (22%)
  starting transfers between devices  17.4 us (4%)
  between operations  15.9 us (4%)
  other arithmetic  15 us (3%)
    all_gather x4, waiting for transfers between devices, body(): lax.all_gather(shared[None, low:low + step], 'seq', axis=0, tiled=True)  133 us
    unnamed x107, local copies, waits for them, and re-layouts  81.6 us
    dot_general x4, matrix products, body(): jnp.einsum('qgd,ld->qgl', chunk_queries, piece[:, 0], preferred_element_t...  38.2 us
    dot_general x4, matrix products, body(): jnp.einsum('qgl,ld->qgd', weights.astype(jnp.bfloat16), piece[:, 1], pref...  29.7 us
    slice x4, local copies, waits for them, and re-layouts, body(): piece[:, 1]  27.4 us
    scatter-add x2, local copies, waits for them, and re-layouts, body(): sums.at[low:]  12.1 us
    all_to_all x1, starting transfers between devices, meet_the_page(): jax.lax.all_to_all(vec_out, split_axis=0, axis_name=ax_name, concat_axis=0)  11.2 us
    all_to_all x1, waiting for transfers between devices, meet_the_page(): jax.lax.all_to_all(vec_out, split_axis=0, axis_name=ax_name, concat_axis=0)  10.6 us
  transfers between devices with their start and end apart: 10, of which 5 were waited for; matrix products, arithmetic and copies ran while one was open for 44% of the time, Pallas kernels for 0%

profile of v1, /device:TPU:1, one launch (start us, length us, event | category | flops | bytes accessed | tf_op | source)
XLA Modules:
  0.0 431.6 jit_solution(17339814584571348226)
XLA Ops:
  6.5 1.4 collective-permute-start.1
  8.0 0.7 slice_bitcast_fusion.70
  8.6 0.8 fusion.109
  9.7 0.9 broadcast_compare_fusion
  10.7 1.6 convert_reduce_fusion
  12.8 6.0 %fusion.57 = f32[512,3,8,88]{0,3,2,1:T(8,128)S(1)} fusion(bf16[3,8,88,1408]{3,2,1,0:T(8,128)(2,1)} %bitcast.436, bf16[512,1408]{1,0:T(8,128)(2,1)S(1)} %copy-done.2, f32[512]{0:T(512)S(1)} %add_rsqrt_fusion.3, f32[512]{0:T(512)S(1)} %broadcast_multiply_fusion), kind=kOutput, calls=%fused_computation.63 | convolution fusion | flops 3047948288 | bytes 11718656 | tf_op jit(solution)/shard_map/dot_general | solution.py:79
  18.8 2.0 copy-done.4
  21.8 4.2 fusion.15
  26.1 3.1 divide_convert_fusion
  29.5 1.2 gather_fusion.2
  31.1 4.3 gather_fusion
  35.4 1.9 gather_fusion.1
  37.3 4.0 fusion.46
  41.6 4.5 %fusion.128 = f32[128,1408]{1,0:T(8,128)S(1)} fusion(bf16[128,2816]{1,0:T(8,128)(2,1)S(1)} %reshape.1031, bf16[2816,1408]{1,0:T(8,128)(2,1)} %bitcast.420), kind=kOutput, calls=%fused_computation.361 | convolution fusion | flops 1015021568 | bytes 9371648 | tf_op jit(solution)/shard_map/dot_general | solution.py:111
  49.2 1.2 add_convert_fusion
  50.7 0.9 fusion.96
  51.7 0.6 constant_dynamic-update-slice_fusion.63
  56.5 0.6 constant_dynamic-update-slice_fusion.55
  67.8 0.6 constant_dynamic-update-slice_fusion.36
  90.0 11.2 %all-to-all-start = ((bf16[64,2,1,1408]{3,1,2,0:T(2,128)(2,1)}), bf16[64,2,1,1408]{3,1,2,0:T(2,128)(2,1)S(1)}, u32[]{:S(2)}, u32[]{:S(2)}) async-start(bf16[64,2,1,1408]{3,1,2,0:T(2,128)(2,1)} %constant_dynamic-update-slice_fusion), calls=%async_computation | async-start | bytes 720896 | tf_op jit(solution)/shard_map/all_to_all | solution.py:124
  101.5 10.6 %all-to-all-done = bf16[64,2,1,1408]{3,1,2,0:T(2,128)(2,1)S(1)} async-done(((bf16[64,2,1,1408]{3,1,2,0:T(2,128)(2,1)}), bf16[64,2,1,1408]{3,1,2,0:T(2,128)(2,1)S(1)}, u32[]{:S(2)}, u32[]{:S(2)}) %all-to-all-start) | async-done | bytes 360480 | tf_op jit(solution)/shard_map/all_to_all | solution.py:124
  112.1 1.6 scatter_fusion
  114.0 1.5 fusion.89
  115.6 0.7 copy.176
  116.4 1.8 collective-permute-start.4
  118.6 0.7 copy.180
  119.7 1.0 compare_and_fusion.3
  120.6 1.3 compare_and_fusion.2
  121.9 0.7 copy.184
  123.6 1.6 compare_and_fusion.1
  125.2 1.9 compare_and_fusion
  127.1 0.8 fusion.98
  128.5 0.8 fusion.91
  129.7 0.8 copy.188
  130.6 47.6 %all-gather.9.cloned.1.call-done = bf16[4096,2,88]{2,1,0:T(2,128)(2,1)} async-done(((bf16[64,2,88]{2,1,0:T(2,128)(2,1)}), bf16[4096,2,88]{2,1,0:T(2,128)(2,1)}) %all-gather.9.cloned.1.call-update) | async-done | bytes 1441808 | tf_op jit(solution)/shard_map/all_gather | solution.py:155
  178.1 6.8 %fusion.126 = (bf16[4096,1,88]{2,1,0:T(2,128)(2,1)}, bf16[4096,1,88]{2,1,0:T(2,128)(2,1)}) fusion(bf16[4096,2,88]{2,1,0:T(2,128)(2,1)} %all-gather.9.cloned.1.call-done), kind=kLoop, calls=%fused_computation.359 | loop fusion | bytes 2883584 | tf_op jit(solution)/shard_map/slice | solution.py:178
  185.0 5.3 %copy.196 = bf16[4096,1,88]{0,2,1:T(8,128)(2,1)} copy(bf16[4096,1,88]{2,1,0:T(2,128)(2,1)} %get-tuple-element.138) | data formatting | bytes 1441792
  190.2 5.3 %copy.197 = bf16[4096,1,88]{0,2,1:T(8,128)(2,1)} copy(bf16[4096,1,88]{2,1,0:T(2,128)(2,1)} %get-tuple-element.137) | data formatting | bytes 1441792
  195.5 48.7 %all-gather.11.cloned.1.call-done = bf16[4096,2,88]{2,1,0:T(2,128)(2,1)} async-done(((bf16[64,2,88]{2,1,0:T(2,128)(2,1)}), bf16[4096,2,88]{2,1,0:T(2,128)(2,1)}) %all-gather.11.cloned.1.call-update) | async-done | bytes 1441808 | tf_op jit(solution)/shard_map/all_gather | solution.py:155
  244.2 6.9 %fusion.125 = (bf16[4096,1,88]{2,1,0:T(2,128)(2,1)}, bf16[4096,1,88]{2,1,0:T(2,128)(2,1)}) fusion(bf16[4096,2,88]{2,1,0:T(2,128)(2,1)} %all-gather.11.cloned.1.call-done), kind=kLoop, calls=%fused_computation.358 | loop fusion | bytes 2883584 | tf_op jit(solution)/shard_map/slice | solution.py:178
  251.1 4.7 %copy.198 = bf16[4096,1,88]{0,2,1:T(8,128)(2,1)S(1)} copy(bf16[4096,1,88]{2,1,0:T(2,128)(2,1)} %get-tuple-element.136) | data formatting | bytes 1441792
  255.8 5.3 %copy.199 = bf16[4096,1,88]{0,2,1:T(8,128)(2,1)} copy(bf16[4096,1,88]{2,1,0:T(2,128)(2,1)} %get-tuple-element.135) | data formatting | bytes 1441792
  261.1 12.1 %fusion.2 = (f32[192,8]{1,0:T(8,128)}, f32[192,8,4096]{2,1,0:T(8,128)}) fusion(pred[192,4096]{1,0:T(8,128)(4,1)S(1)} %copy-done.7, bf16[256,8,88]{2,1,0:T(8,128)(2,1)S(1)} %multiply_convert_fusion.2, bf16[4096,1,88]{0,2,1:T(8,128)(2,1)S(1)} %copy.198), kind=kOutput, calls=%fused_computation.8 | convolution fusion | flops 1126169088 | bytes 27039744 | tf_op jit(solution)/shard_map/qgd,ld->qgl/dot_general | solution.py:164
  273.2 10.5 %fusion.9 = f32[192,8,88]{2,1,0:T(8,128)S(1)} fusion(f32[192,8,4096]{2,1,0:T(8,128)} %get-tuple-element.158, pred[192,4096]{1,0:T(8,128)(4,1)S(1)} %copy-done.7, bf16[4096,1,88]{0,2,1:T(8,128)(2,1)} %copy.199), kind=kOutput, calls=%fused_computation.15 | convolution fusion | flops 1126170624 | bytes 27213824 | tf_op jit(solution)/shard_map/qgl,ld->qgd/dot_general | solution.py:175
  284.1 16.5 %fusion = (f32[256,8]{0,1:T(8,128)S(1)}, f32[256,8,4096]{2,0,1:T(8,128)}) fusion(pred[256,4096]{1,0:T(8,128)(4,1)} %compare_and_fusion, bf16[256,8,88]{0,2,1:T(8,128)(2,1)} %bitcast.428, bf16[4096,1,88]{0,2,1:T(8,128)(2,1)} %copy.196), kind=kOutput, calls=%fused_computation.5 | convolution fusion | flops 1501558784 | bytes 35692544 | tf_op jit(solution)/shard_map/qgd,ld->qgl/dot_general | solution.py:164
  300.6 13.8 %fusion.4 = f32[256,8,88]{0,2,1:T(8,128)S(1)} fusion(f32[256,8,4096]{2,0,1:T(8,128)} %get-tuple-element.156, pred[256,4096]{1,0:T(8,128)(4,1)S(1)} %copy-done.6, bf16[4096,1,88]{0,2,1:T(8,128)(2,1)S(1)} %copy-done.9), kind=kOutput, calls=%fused_computation.11 | convolution fusion | flops 1501560832 | bytes 36044800 | tf_op jit(solution)/shard_map/qgl,ld->qgd/dot_general | solution.py:175
  314.7 7.1 %scatter-add.20 = f32[256,8,88]{0,2,1:T(8,128)S(1)} dynamic-update-slice(f32[256,8,88]{0,2,1:T(8,128)S(1)} %fusion.4, f32[192,8,88]{0,2,1:T(8,128)S(1)} %slice_add_fusion, s32[]{:T(128)} %constant.358.clone.1, s32[]{:T(128)} %constant.360.clone.1, s32[]{:T(128)} %constant.360.clone.1) | dynamic-update-slice | bytes 1081348 | tf_op jit(solution)/shard_map/scatter-add | solution.py:174
  321.8 7.0 %fusion.124 = (bf16[4096,1,88]{2,1,0:T(2,128)(2,1)}, bf16[4096,1,88]{2,1,0:T(2,128)(2,1)}) fusion(bf16[4096,2,88]{2,1,0:T(2,128)(2,1)} %all-gather.13.cloned.1.call-done), kind=kLoop, calls=%fused_computation.357 | loop fusion | bytes 2883584 | tf_op jit(solution)/shard_map/slice | solution.py:178
  328.8 5.3 %copy.201 = bf16[4096,1,88]{0,2,1:T(8,128)(2,1)} copy(bf16[4096,1,88]{2,1,0:T(2,128)(2,1)} %get-tuple-element.133) | data formatting | bytes 1441792
  334.0 5.3 %copy.200 = bf16[4096,1,88]{0,2,1:T(8,128)(2,1)} copy(bf16[4096,1,88]{2,1,0:T(2,128)(2,1)} %get-tuple-element.134) | data formatting | bytes 1441792
  339.4 36.9 %all-gather.15.cloned.1.call-done = bf16[4096,2,88]{2,1,0:T(2,128)(2,1)} async-done(((bf16[64,2,88]{2,1,0:T(2,128)(2,1)}), bf16[4096,2,88]{2,1,0:T(2,128)(2,1)}) %all-gather.15.cloned.1.call-update) | async-done | bytes 1441808 | tf_op jit(solution)/shard_map/all_gather | solution.py:155
  376.3 6.8 %fusion.123 = (bf16[4096,1,88]{2,1,0:T(2,128)(2,1)}, bf16[4096,1,88]{2,1,0:T(2,128)(2,1)}) fusion(bf16[4096,2,88]{2,1,0:T(2,128)(2,1)} %all-gather.15.cloned.1.call-done), kind=kLoop, calls=%fused_computation.356 | loop fusion | bytes 2883584 | tf_op jit(solution)/shard_map/slice | solution.py:178
  383.0 4.6 %copy.202 = bf16[4096,1,88]{0,2,1:T(8,128)(2,1)S(1)} copy(bf16[4096,1,88]{2,1,0:T(2,128)(2,1)} %get-tuple-element.132) | data formatting | bytes 1441792
  387.7 5.3 %copy.203 = bf16[4096,1,88]{0,2,1:T(8,128)(2,1)} copy(bf16[4096,1,88]{2,1,0:T(2,128)(2,1)} %get-tuple-element.131) | data formatting | bytes 1441792
  393.0 3.9 fusion.17
  396.9 2.5 fusion.23
  399.5 1.1 copy.191
  401.0 5.7 %fusion.7 = (f32[128,8]{0,1:T(8,128)S(1)}, f32[128,8,4096]{2,0,1:T(8,128)S(1)}) fusion(pred[128,4096]{1,0:T(8,128)(4,1)S(1)} %copy-done.11, bf16[4096,1,88]{0,2,1:T(8,128)(2,1)} %copy.200, bf16[128,8,88]{2,1,0:T(8,128)(2,1)S(1)} %slice-done), kind=kOutput, calls=%fused_computation.13 | convolution fusion | flops 750779392 | bytes 18206720 | tf_op jit(solution)/shard_map/qgd,ld->qgl/dot_general | solution.py:164
  406.8 2.8 constant_dynamic-update-slice_fusion.65
  409.8 5.0 %scatter-add.24 = f32[256,8,88]{0,2,1:T(8,128)S(1)} dynamic-update-slice(f32[256,8,88]{0,2,1:T(8,128)S(1)} %get-tuple-element.153, f32[64,8,88]{0,2,1:T(8,128)S(1)} %slice_add_fusion.1, s32[]{:T(128)} %constant.377.clone.1, s32[]{:T(128)} %constant.360.clone.1, s32[]{:T(128)} %constant.360.clone.1) | dynamic-update-slice | bytes 360452 | tf_op jit(solution)/shard_map/scatter-add | solution.py:174
  415.2 0.7 copy-done.12
  415.9 1.6 collective-permute-start.3
  417.5 1.3 collective-permute-done.3
  418.9 6.0 %fusion.50 = bf16[256,1,1408]{2,0,1:T(8,128)(2,1)} fusion(bf16[704,1408]{1,0:T(8,128)(2,1)} %collective-permute-done.4, bf16[704,1408]{1,0:T(8,128)(2,1)} %param.43, pred[]{:T(512)S(6)} %eq.136, bf16[256,1408]{1,0:T(8,128)(2,1)S(1)} %scatter_fusion, bf16[256,704]{0,1:T(8,128)(2,1)S(1)} %collective-permute-done.3, bf16[256,704]{0,1:T(8,128)(2,1)} %bitcast.430), kind=kOutput, calls=%fused_computation.55 | convolution fusion | flops 1037189120 | bytes 6127617 | tf_op jit(solution)/shard_map/dot_general | solution.py:184
  (189 shorter events, 45.6 us)
Async XLA Ops:
  6.5 120.6 %copy-start = (bf16[1408,704]{0,1:T(8,128)(2,1)S(1)}, bf16[1408,704]{0,1:T(8,128)(2,1)}, u32[]{:S(2)}) copy-start(bf16[1408,704]{0,1:T(8,128)(2,1)} %param.41) | copy-start | bytes 5947396
  6.5 5.8 %copy-start.2 = (bf16[512,1408]{1,0:T(8,128)(2,1)S(1)}, bf16[512,1408]{1,0:T(8,128)(2,1)}, u32[]{:S(2)}) copy-start(bf16[512,1408]{1,0:T(8,128)(2,1)} %param.32) | copy-start | bytes 4325380
  6.5 30.8 %collective-permute-start.1 = (bf16[704,1408]{1,0:T(8,128)(2,1)}, bf16[704,1408]{1,0:T(8,128)(2,1)}, u32[]{:S(2)}, u32[]{:S(2)}) collective-permute-start(bf16[704,1408]{1,0:T(8,128)(2,1)} %param.39), channel_id=1, source_target_pairs={{0,64},{64,0},{1,65},{65,1},{2,66},{66,2},{3,67},{67,3},{4,68},{68... | collective-permute-start | bytes 5947400 | tf_op jit(solution)/shard_map/ppermute | solution.py:45
  18.8 2.0 copy-start.4
  21.8 4.2 copy-start.15
  30.7 6.6 %collective-permute-start = (bf16[256,704]{1,0:T(8,128)(2,1)S(1)}, bf16[256,704]{1,0:T(8,128)(2,1)}, u32[]{:S(2)}, u32[]{:S(2)}) collective-permute-start(bf16[256,704]{1,0:T(8,128)(2,1)S(1)} %gather_fusion.2), channel_id=1, source_target_pairs={{0,64},{64,0},{1,65},{65,1},{2,66},{66,2},{3,67},{67,3},{4,68},{68... | collective-permute-start | bytes 1081352 | tf_op jit(solution)/shard_map/ppermute | solution.py:45
  41.5 5.0 %copy-start.17 = (s32[8192]{0:T(1024)S(1)}, s32[8192]{0:T(1024)}, u32[]{:S(2)}) copy-start(s32[8192]{0:T(1024)} %param.35) | copy-start | bytes 98308
  46.1 66.0 %copy-start.3 = (bf16[256,1,1408]{2,0,1:T(8,128)(2,1)S(1)}, bf16[256,1,1408]{2,0,1:T(8,128)(2,1)}, u32[]{:S(2)}) copy-start(bf16[256,1,1408]{2,0,1:T(8,128)(2,1)} %param.36) | copy-start | bytes 2162692
  46.1 3.0 collective-permute-start.2
  90.0 22.1 %all-to-all-start = ((bf16[64,2,1,1408]{3,1,2,0:T(2,128)(2,1)}), bf16[64,2,1,1408]{3,1,2,0:T(2,128)(2,1)S(1)}, u32[]{:S(2)}, u32[]{:S(2)}) async-start(bf16[64,2,1,1408]{3,1,2,0:T(2,128)(2,1)} %constant_dynamic-update-slice_fusion), calls=%async_computation | async-start | bytes 720896 | tf_op jit(solution)/shard_map/all_to_all | solution.py:124
  101.2 76.9 %all-gather.9.cloned.1.call-start = ((), (), s32[]{:S(2)}) async-start(), calls=%async_computation.1 | async-start | bytes 2129920 | tf_op jit(solution)/shard_map/all_gather | solution.py:155
  112.1 6.1 %copy-start.13 = (s32[256,64]{0,1:T(8,128)S(1)}, s32[256,64]{0,1:T(8,128)}, u32[]{:S(2)}) copy-start(s32[256,64]{0,1:T(8,128)} %param.37) | copy-start | bytes 196612
  116.4 127.8 %all-gather.11.cloned.1.call-start = ((), (), s32[]{:S(2)}) async-start(), calls=%async_computation.2 | async-start | bytes 2129920 | tf_op jit(solution)/shard_map/all_gather | solution.py:155
  116.4 301.1 %collective-permute-start.4 = (bf16[704,1408]{1,0:T(8,128)(2,1)}, bf16[704,1408]{1,0:T(8,128)(2,1)}, u32[]{:S(2)}, u32[]{:S(2)}) collective-permute-start(bf16[704,1408]{1,0:T(8,128)(2,1)} %param.43), channel_id=1, source_target_pairs={{0,64},{64,0},{1,65},{65,1},{2,66},{66,2},{3,67},{67,3},{4,68},{68... | collective-permute-start | bytes 5947400 | tf_op jit(solution)/shard_map/ppermute | solution.py:45
  119.3 202.5 %all-gather.13.cloned.1.call-start = ((), (), s32[]{:S(2)}) async-start(), calls=%async_computation.3 | async-start | bytes 2129920 | tf_op jit(solution)/shard_map/all_gather | solution.py:155
  122.6 253.6 %all-gather.15.cloned.1.call-start = ((), (), s32[]{:S(2)}) async-start(), calls=%async_computation.4 | async-start | bytes 2129920 | tf_op jit(solution)/shard_map/all_gather | solution.py:155
  129.7 263.2 %copy-start.5 = (bf16[256,8,88]{2,1,0:T(8,128)(2,1)}, bf16[256,8,88]{2,1,0:T(8,128)(2,1)S(1)}, u32[]{:S(2)}) copy-start(bf16[256,8,88]{2,1,0:T(8,128)(2,1)S(1)} %multiply_convert_fusion.2) | copy-start | bytes 1081348
  251.1 10.0 %copy-start.7 = (pred[192,4096]{1,0:T(8,128)(4,1)S(1)}, pred[192,4096]{1,0:T(8,128)(4,1)}, u32[]{:S(2)}) copy-start(pred[192,4096]{1,0:T(8,128)(4,1)} %compare_and_fusion.1) | copy-start | bytes 2359300
  284.1 16.5 %copy-start.6 = (pred[256,4096]{1,0:T(8,128)(4,1)S(1)}, pred[256,4096]{1,0:T(8,128)(4,1)}, u32[]{:S(2)}) copy-start(pred[256,4096]{1,0:T(8,128)(4,1)} %compare_and_fusion) | copy-start | bytes 3145732
  284.1 16.5 %copy-start.9 = (bf16[4096,1,88]{0,2,1:T(8,128)(2,1)S(1)}, bf16[4096,1,88]{0,2,1:T(8,128)(2,1)}, u32[]{:S(2)}) copy-start(bf16[4096,1,88]{0,2,1:T(8,128)(2,1)} %copy.197) | copy-start | bytes 2162692
  393.0 3.9 copy-start.10
  393.0 3.9 copy-start.14
  396.9 3.7 copy-start.16
  396.9 4.1 slice-start
  396.9 4.1 copy-start.11
  401.0 5.7 %copy-start.8 = (bf16[4096,1,88]{0,2,1:T(8,128)(2,1)S(1)}, bf16[4096,1,88]{0,2,1:T(8,128)(2,1)}, u32[]{:S(2)}) copy-start(bf16[4096,1,88]{0,2,1:T(8,128)(2,1)} %copy.201) | copy-start | bytes 2162692
  415.2 0.7 copy-start.12
  415.9 2.9 collective-permute-start.3
  418.8 6.0 %copy-start.1 = (bf16[1408,704]{0,1:T(8,128)(2,1)S(1)}, bf16[1408,704]{0,1:T(8,128)(2,1)}, u32[]{:S(2)}) copy-start(bf16[1408,704]{0,1:T(8,128)(2,1)} %param.41) | copy-start | bytes 5947396
Sparse Core Ops, SparseCore 0:
  116.5 61.5 all-gather.8
  181.0 63.1 all-gather.10
  247.1 63.1 all-gather.12
  313.0 63.1 all-gather.14
